TPU v7x, 32 devices: a whole 2x2x4 slice. The times are simulated.
32 devices in a mesh: pb: 8 (over z, y), col: 4 (over x, core).
Axes of the slice: x: 2, y: 2, z: 4, core: 2. Of those that a mesh axis runs over, the one named last changes fastest.
Arguments:
- orbitals: bfloat16 [8, 48, 4096], P('pb', None, 'col'), may hold values from -6 to 6
- screening: bfloat16 [8, 4096, 4096], P('pb', None, 'col'), may hold values from -0.0014648438 to 0.0014648438
- pairs_k: int32 [8, 4], P('pb'), may hold values from 0 to 7
Outputs:
- kernel: float32 [8, 4, 256, 1024], P('pb', None, None, 'col')
All inputs are finite; a program needn't handle non-finite values.
Results may differ from a plain program's by a relative error of at most 0.0049.
Values may be sent and summed in bfloat16 or wider, within the bound.
No kernel may reach another device: no remote copies, remote signals or barrier semaphores. Data moves between devices by JAX's collectives and lax.ppermute only.
A program may use at most 128 MiB of HBM per device.

v0:
```python
import jax
import jax.numpy as jnp
from jax import lax
from jax.sharding import PartitionSpec as P

NV = 16
NC = 32


def body(orbitals, screening, pairs_k):
    k_dev, orb_count, mu_cols = orbitals.shape
    group_count = lax.axis_size("pb")
    kpoint_count = k_dev * group_count
    group_index = lax.axis_index("pb")
    kpoint_a = pairs_k[0]
    kpoint_b = (kpoint_a - group_index) % kpoint_count
    wanted = jnp.concatenate([kpoint_a, kpoint_b])
    slot_count = wanted.shape[0]
    pair_count = slot_count // 2
    block_rows = lax.all_gather(orbitals, "pb", axis=0, tiled=True)
    indices = jnp.arange(block_rows.shape[0], dtype=jnp.int32)
    chooser = (wanted[:, None] == indices[None, :]).astype(jnp.bfloat16)
    fetched = jnp.einsum(
        "sk,kom->som", chooser, block_rows, preferred_element_type=jnp.float32
    ).astype(jnp.bfloat16)
    valence = lax.all_gather(fetched[:, :NV, :], "col", axis=2, tiled=True)
    valence_a = valence[:pair_count].astype(jnp.float32)
    valence_b = valence[pair_count:].astype(jnp.float32)
    val_pairs = (valence_a[:, :, None, :] * valence_b[:, None, :, :]).astype(jnp.bfloat16)
    val_pairs = val_pairs.reshape(pair_count * NV * NV, valence.shape[2])
    screened = jnp.dot(val_pairs, screening[0], preferred_element_type=jnp.float32).astype(
        jnp.bfloat16
    )
    screened = screened.reshape(pair_count, NV * NV, mu_cols)
    conduction = fetched[:, NV:, :].astype(jnp.float32)
    cond_pairs = (conduction[:pair_count, :, None, :] * conduction[pair_count:, None, :, :]).astype(
        jnp.bfloat16
    )
    cond_pairs = cond_pairs.reshape(pair_count, NC * NC, mu_cols)
    partial_value = jnp.einsum(
        "pan,pbn->pab", screened, cond_pairs, preferred_element_type=jnp.float32
    )
    whole_sum = lax.psum(partial_value, "col")
    column_count = whole_sum.shape[2] // lax.axis_size("col")
    result = lax.dynamic_slice_in_dim(
        whole_sum, lax.axis_index("col") * column_count, column_count, 2
    )
    return result[None]


def solution(mesh):
    placed = (P("pb", None, "col"), P("pb", None, "col"), P("pb", None))
    return jax.shard_map(
        body, mesh=mesh, in_specs=placed, out_specs=P("pb", None, None, "col"), check_vma=False
    )
```

profile of v0, /device:TPU:0, one launch (start us, length us, event | category | flops | bytes accessed | tf_op | source)
XLA Modules:
  0.0 181.1 jit_solution(12685223790277849974)
XLA Ops:
  6.5 0.0 all-gather.2.cloned.1.call-start
  6.5 34.0 %all_gather.6 = bf16[8,48,1024]{2,1,0:T(8,128)(2,1)S(1)} all-gather(bf16[1,48,1024]{2,1,0:T(8,128)(2,1)} %param.3), channel_id=1, replica_groups=mesh['pb'=8,'col'=4] {'pb'}, dimensions={0}, use_global_device_ids=true | all-gather | bytes 884736 | tf_op jit(solution)/shard_map/all_gather | solution.py:20
  40.5 0.7 and_select_fusion
  41.2 0.7 pad_add_fusion
  41.9 0.6 fusion.5
  42.5 0.4 copy.19
  42.9 0.7 slice.24
  43.6 0.0 all-gather.2.cloned.1.call-update
  43.7 0.0 all-reduce.2.cloned.1.call-start
  43.7 0.1 slice_convert_fusion
  43.8 0.1 fusion.11
  43.9 6.2 %multiply_convert_fusion = bf16[4,32,32,1024]{3,2,1,0:T(8,128)(2,1)} fusion(f32[4,32,1024]{2,1,0:T(8,128)S(1)} %get-tuple-element.6, f32[4,32,1024]{2,1,0:T(8,128)S(1)} %get-tuple-element.5), kind=kLoop, calls=%fused_computation | loop fusion | flops 8388608 | bytes 9437184 | tf_op jit(solution)/shard_map/convert_element_type | solution.py:36
  50.2 11.4 %all-gather.2.cloned.1.call-done = bf16[8,16,4096]{2,1,0:T(8,128)(2,1)} async-done(((bf16[8,16,1024]{2,1,0:T(8,128)(2,1)}), bf16[8,16,4096]{2,1,0:T(8,128)(2,1)}) %all-gather.2.cloned.1.call-update) | async-done | bytes 1048592 | tf_op jit(solution)/shard_map/all_gather | solution.py:26
  61.6 1.4 slice_convert_fusion.2
  63.0 0.0 slice-start
  63.0 5.2 %multiply_convert_fusion.1 = bf16[4,16,16,4096]{3,2,1,0:T(8,128)(2,1)} fusion(f32[4,16,4096]{2,1,0:T(8,128)S(1)} %get-tuple-element.8, f32[4,16,4096]{2,1,0:T(8,128)S(1)} %get-tuple-element.7), kind=kLoop, calls=%fused_computation.1 | loop fusion | flops 8388608 | bytes 10485760 | tf_op jit(solution)/shard_map/convert_element_type | solution.py:29
  68.2 0.0 slice-start.1
  68.2 13.8 %fusion.2 = bf16[1024,1024]{1,0:T(8,128)(2,1)S(1)} fusion(bf16[1024,4096]{1,0:T(8,128)(2,1)} %bitcast.21, bf16[1,4096,1024]{2,1,0:T(8,128)(2,1)} %param.4), kind=kOutput, calls=%fused_computation.4 | convolution fusion | flops 8590983168 | bytes 18874368 | tf_op jit(solution)/shard_map/dot_general | solution.py:31
  82.0 0.0 slice-done
  82.0 0.0 slice-done.1
  82.0 4.4 %fusion.12 = f32[4,256,1024]{2,1,0:T(8,128)} fusion(bf16[4,256,1024]{2,1,0:T(8,128)(2,1)S(1)} %bitcast.22, bf16[4,1024,1024]{2,1,0:T(8,128)(2,1)S(1)} %bitcast.20), kind=kOutput, calls=%fused_computation.21 | convolution fusion | flops 2147483648 | bytes 14680064 | tf_op jit(solution)/shard_map/pan,pbn->pab/dot_general | solution.py:40
  86.4 0.0 all-reduce.2.cloned.1.call-update
  86.4 85.6 %all-reduce.2.cloned.1.call-done = f32[4,256,1024]{2,1,0:T(8,128)} async-done(((f32[4,256,1024]{2,1,0:T(8,128)}), f32[4,256,1024]{2,1,0:T(8,128)}) %all-reduce.2.cloned.1.call-update) | async-done | bytes 4194320 | tf_op jit(solution)/shard_map/psum | solution.py:43
  172.0 2.3 %dynamic-slice_bitcast_fusion = f32[1,4,256,256]{3,2,1,0:T(8,128)} fusion(f32[4,256,1024]{2,1,0:T(8,128)} %all-reduce.2.cloned.1.call-done, s32[]{:T(128)S(6)} %select_n.11), kind=kLoop, calls=%fused_computation.6 | loop fusion | bytes 2097156 | tf_op jit(solution)/shard_map/broadcast_in_dim | solution.py:48
  (1 shorter events, 0.0 us)
Async XLA Ops:
  6.5 55.0 %all-gather.2.cloned.1.call-start = ((), (), s32[]{:S(2)}) async-start(), calls=%async_computation | async-start | bytes 1310720 | tf_op jit(solution)/shard_map/all_gather | solution.py:26
  43.7 128.3 %all-reduce.2.cloned.1.call-start = ((), (), s32[]{:S(2)}) async-start(), calls=%async_computation.1 | async-start | bytes 8388608 | tf_op jit(solution)/shard_map/psum | solution.py:43
  63.0 19.0 %slice-start = ((s8[8388608]{0:T(1024)(128)(4,1)}), s8[4194304]{0:T(1024)(128)(4,1)S(1)}, s32[]{:S(2)}) async-start(s8[8388608]{0:T(1024)(128)(4,1)} %bitcast.18), calls=%async_computation.2 | async-start | bytes 8388608
  68.2 13.8 %slice-start.1 = ((s8[8388608]{0:T(1024)(128)(4,1)}), s8[4194304]{0:T(1024)(128)(4,1)S(1)}, s32[]{:S(2)}) async-start(s8[8388608]{0:T(1024)(128)(4,1)} %bitcast.18), calls=%async_computation.3 | async-start | bytes 8388608
Sparse Core Ops, SparseCore 0:
  43.8 17.7 all-gather.1
  86.5 85.4 all-reduce.1
where the time goes:
time: 181 us
  waiting for transfers between devices  97 us (54%)
  blocking collectives  34 us (19%)
  matrix products  18.7 us (10%)
  other arithmetic  14.3 us (8%)
  between operations  13.5 us (7%)
  local copies, waits for them, and re-layouts  3.56 us (2%)
    psum x1, waiting for transfers between devices, body(): whole_sum = lax.psum(partial_value, 'col')  85.6 us
    all_gather x1, blocking collectives, body(): block_rows = lax.all_gather(orbitals, 'pb', axis=0, tiled=True)  34 us
    dot_general x1, matrix products, body(): jnp.dot(val_pairs, screening[0], preferred_element_type=jnp.float32)  13.8 us
    all_gather x1, waiting for transfers between devices, body(): valence = lax.all_gather(fetched[:, :NV, :], 'col', axis=2, tiled=True)  11.4 us
    convert_element_type x1, other arithmetic, body(): (conduction[:pair_count, :, None, :] * conduction[pair_count:, None, :, :...  6.24 us
    convert_element_type x1, other arithmetic, body(): (valence_a[:, :, None, :] * valence_b[:, None, :, :]).astype(jnp.bfloat16)  5.17 us
    dot_general x1, matrix products, body(): jnp.einsum('pan,pbn->pab', screened, cond_pairs, preferred_element_type=j...  4.36 us
  transfers between devices with their start and end apart: 2, of which 2 were waited for; matrix products, arithmetic and copies ran while one was open for 4% of the time, Pallas kernels for 0%

commit v1 on v0

--- a/solution.py
+++ b/solution.py
@@ -40,7 +40,7 @@
     partial_value = jnp.einsum(
         "pan,pbn->pab", screened, cond_pairs, preferred_element_type=jnp.float32
     )
-    whole_sum = lax.psum(partial_value, "col")
+    whole_sum = jnp.sum(lax.all_gather(partial_value, "col"), axis=0)
     column_count = whole_sum.shape[2] // lax.axis_size("col")
     result = lax.dynamic_slice_in_dim(
         whole_sum, lax.axis_index("col") * column_count, column_count, 2

time: 181 us -> 212 us (1.17)
  waiting for transfers between devices: 97 us -> 118 us
  other arithmetic: 14.3 us -> 24.6 us
    all_gather x0 -> x1, waiting for transfers between devices: none -> 106 us  [body(): whole_sum = jnp.sum(lax.all_gather(partial_value, 'col'), axis=0)]
    psum x1 -> x0, waiting for transfers between devices: 85.6 us -> none  [body(): whole_sum = lax.psum(partial_value, 'col')]
    reduce_sum x0 -> x1, other arithmetic: none -> 10.3 us  [body(): whole_sum = jnp.sum(lax.all_gather(partial_value, 'col'), axis=0)]
  transfers between devices with their start and end apart: 2 -> 2, of which waited for: 2 -> 2; matrix products, arithmetic and copies ran while one was open for 4% -> 3% of each run, Pallas kernels for 0% -> 0%
where the time goes in v1:
time: 212 us
  waiting for transfers between devices  118 us (56%)
  blocking collectives  34 us (16%)
  other arithmetic  24.6 us (12%)
  matrix products  18.7 us (9%)
  between operations  13.5 us (6%)
  local copies, waits for them, and re-layouts  3.56 us (2%)
    all_gather x1, waiting for transfers between devices, body(): whole_sum = jnp.sum(lax.all_gather(partial_value, 'col'), axis=0)  106 us
    all_gather x1, blocking collectives, body(): block_rows = lax.all_gather(orbitals, 'pb', axis=0, tiled=True)  34 us
    dot_general x1, matrix products, body(): jnp.dot(val_pairs, screening[0], preferred_element_type=jnp.float32)  13.8 us
    all_gather x1, waiting for transfers between devices, body(): valence = lax.all_gather(fetched[:, :NV, :], 'col', axis=2, tiled=True)  11.4 us
    reduce_sum x1, other arithmetic, body(): whole_sum = jnp.sum(lax.all_gather(partial_value, 'col'), axis=0)  10.3 us
    convert_element_type x1, other arithmetic, body(): (conduction[:pair_count, :, None, :] * conduction[pair_count:, None, :, :...  6.24 us
    convert_element_type x1, other arithmetic, body(): (valence_a[:, :, None, :] * valence_b[:, None, :, :]).astype(jnp.bfloat16)  5.17 us
    dot_general x1, matrix products, body(): jnp.einsum('pan,pbn->pab', screened, cond_pairs, preferred_element_type=j...  4.33 us
  transfers between devices with their start and end apart: 2, of which 2 were waited for; matrix products, arithmetic and copies ran while one was open for 3% of the time, Pallas kernels for 0%

profile of v1, /device:TPU:0, one launch (start us, length us, event | category | flops | bytes accessed | tf_op | source)
XLA Modules:
  0.0 211.8 jit_solution(11526990211560439759)
XLA Ops:
  6.5 0.0 all-gather.4.cloned.1.call-start
  6.5 34.0 %all_gather.12 = bf16[8,48,1024]{2,1,0:T(8,128)(2,1)S(1)} all-gather(bf16[1,48,1024]{2,1,0:T(8,128)(2,1)} %param.3), channel_id=1, replica_groups=mesh['pb'=8,'col'=4] {'pb'}, dimensions={0}, use_global_device_ids=true | all-gather | bytes 884736 | tf_op jit(solution)/shard_map/all_gather | solution.py:20
  40.5 0.7 and_select_fusion
  41.2 0.7 pad_add_fusion
  41.9 0.6 fusion.5
  42.5 0.4 copy.19
  42.9 0.7 slice.24
  43.6 0.0 all-gather.4.cloned.1.call-update
  43.7 0.0 all-gather.6.cloned.1.call-start
  43.7 0.1 slice_convert_fusion
  43.8 0.1 fusion.11
  43.9 6.2 %multiply_convert_fusion = bf16[4,32,32,1024]{3,2,1,0:T(8,128)(2,1)} fusion(f32[4,32,1024]{2,1,0:T(8,128)S(1)} %get-tuple-element.6, f32[4,32,1024]{2,1,0:T(8,128)S(1)} %get-tuple-element.5), kind=kLoop, calls=%fused_computation | loop fusion | flops 8388608 | bytes 9437184 | tf_op jit(solution)/shard_map/convert_element_type | solution.py:36
  50.2 11.4 %all-gather.4.cloned.1.call-done = bf16[8,16,4096]{2,1,0:T(8,128)(2,1)} async-done(((bf16[8,16,1024]{2,1,0:T(8,128)(2,1)}), bf16[8,16,4096]{2,1,0:T(8,128)(2,1)}) %all-gather.4.cloned.1.call-update) | async-done | bytes 1048592 | tf_op jit(solution)/shard_map/all_gather | solution.py:26
  61.6 1.4 slice_convert_fusion.2
  63.0 0.0 slice-start
  63.0 5.2 %multiply_convert_fusion.1 = bf16[4,16,16,4096]{3,2,1,0:T(8,128)(2,1)} fusion(f32[4,16,4096]{2,1,0:T(8,128)S(1)} %get-tuple-element.8, f32[4,16,4096]{2,1,0:T(8,128)S(1)} %get-tuple-element.7), kind=kLoop, calls=%fused_computation.1 | loop fusion | flops 8388608 | bytes 10485760 | tf_op jit(solution)/shard_map/convert_element_type | solution.py:29
  68.2 0.0 slice-start.1
  68.2 13.8 %fusion.2 = bf16[1024,1024]{1,0:T(8,128)(2,1)S(1)} fusion(bf16[1024,4096]{1,0:T(8,128)(2,1)} %bitcast.23, bf16[1,4096,1024]{2,1,0:T(8,128)(2,1)} %param.4), kind=kOutput, calls=%fused_computation.4 | convolution fusion | flops 8590983168 | bytes 18874368 | tf_op jit(solution)/shard_map/dot_general | solution.py:31
  82.0 0.0 slice-done
  82.0 0.0 slice-done.1
  82.0 4.3 %fusion.12 = f32[4,256,1024]{2,1,0:T(8,128)} fusion(bf16[4,256,1024]{2,1,0:T(8,128)(2,1)S(1)} %bitcast.24, bf16[4,1024,1024]{2,1,0:T(8,128)(2,1)S(1)} %bitcast.21), kind=kOutput, calls=%fused_computation.21 | convolution fusion | flops 2147483648 | bytes 14680064 | tf_op jit(solution)/shard_map/pan,pbn->pab/dot_general | solution.py:40
  86.3 0.0 all-gather.6.cloned.1.call-update
  86.4 106.1 %all-gather.6.cloned.1.call-done = f32[16,256,1024]{2,1,0:T(8,128)} async-done(((f32[4,256,1024]{2,1,0:T(8,128)}), f32[16,256,1024]{2,1,0:T(8,128)}) %all-gather.6.cloned.1.call-update) | async-done | bytes 16777232 | tf_op jit(solution)/shard_map/all_gather | solution.py:43
  192.4 10.3 %reduce_sum.9 = f32[4,256,1024]{2,1,0:T(8,128)} reduce(f32[4,4,256,1024]{3,2,1,0:T(8,128)} %bitcast.22, f32[]{:T(128)} %constant.27.clone.1), dimensions={0}, to_apply=%region_0.1 | reduce | flops 3145728 | bytes 20971524 | tf_op jit(solution)/shard_map/reduce_sum | solution.py:43
  202.7 2.3 %dynamic-slice_bitcast_fusion = f32[1,4,256,256]{3,2,1,0:T(8,128)} fusion(f32[4,256,1024]{2,1,0:T(8,128)} %reduce_sum.9, s32[]{:T(128)S(6)} %select_n.11), kind=kLoop, calls=%fused_computation.6 | loop fusion | bytes 2097156 | tf_op jit(solution)/shard_map/broadcast_in_dim | solution.py:48
  (1 shorter events, 0.0 us)
Async XLA Ops:
  6.5 55.0 %all-gather.4.cloned.1.call-start = ((), (), s32[]{:S(2)}) async-start(), calls=%async_computation | async-start | bytes 1310720 | tf_op jit(solution)/shard_map/all_gather | solution.py:26
  43.7 148.8 %all-gather.6.cloned.1.call-start = ((), (), s32[]{:S(2)}) async-start(), calls=%async_computation.1 | async-start | bytes 20971520 | tf_op jit(solution)/shard_map/all_gather | solution.py:43
  63.0 19.0 %slice-start = ((s8[8388608]{0:T(1024)(128)(4,1)}), s8[4194304]{0:T(1024)(128)(4,1)S(1)}, s32[]{:S(2)}) async-start(s8[8388608]{0:T(1024)(128)(4,1)} %bitcast.19), calls=%async_computation.2 | async-start | bytes 8388608
  68.2 13.8 %slice-start.1 = ((s8[8388608]{0:T(1024)(128)(4,1)}), s8[4194304]{0:T(1024)(128)(4,1)S(1)}, s32[]{:S(2)}) async-start(s8[8388608]{0:T(1024)(128)(4,1)} %bitcast.19), calls=%async_computation.3 | async-start | bytes 8388608
Sparse Core Ops, SparseCore 0:
  43.8 17.7 all-gather.3
  86.5 105.9 all-gather.5
